TPU v7x, 256 devices: a whole 4x4x8 slice. The times are simulated.
256 devices in a mesh: dp: 4 (over z_hi, core), ctx: 64 (over x, z_lo, y).
Axes of the slice: x: 4, y: 4, z: 8 (z_hi: 2, z_lo: 4; z = z_hi * 4 + z_lo), core: 2. Of those that a mesh axis runs over, the one named last changes fastest.
Arguments:
- query_rows: bfloat16 [4, 16384, 2048], P('dp', 'ctx'), may hold values from -40 to 40
- key_rows: bfloat16 [4, 16384, 1024], P('dp', 'ctx'), may hold values from -6 to 6
- value_rows: bfloat16 [4, 16384, 1024], P('dp', 'ctx'), may hold values from -6 to 6
- out_grad: bfloat16 [4, 16384, 2048], P('dp', 'ctx'), may hold values from -6 to 6
- gate_grads: bfloat16 [4, 18432, 2304], P('dp', 'ctx'), may hold values from -6 to 6
- first_moment: float32 [18432, 2304], P('ctx', 'dp'), may hold values from -3 to 3
- second_moment: float32 [18432, 2304], P('ctx', 'dp'), may hold values from 0.05 to 2
- master_rows: float32 [18432, 2304], P('ctx', 'dp'), may hold values from -3 to 3
Outputs:
- query_grad: bfloat16 [4, 16384, 2048], P('dp', 'ctx')
- key_grad: bfloat16 [4, 16384, 1024], P('dp', 'ctx')
- value_grad: bfloat16 [4, 16384, 1024], P('dp', 'ctx')
- gate_params: bfloat16 [18432, 2304], P('ctx')
- new_first: float32 [18432, 2304], P('ctx', 'dp')
- new_second: float32 [18432, 2304], P('ctx', 'dp')
- new_master: float32 [18432, 2304], P('ctx', 'dp')
All inputs are finite; a program needn't handle non-finite values.
Results may differ from a plain program's by a relative error of at most 0.019.
Values may be sent and summed in bfloat16 or wider, within the bound.
No kernel may reach another device: no remote copies, remote signals or barrier semaphores. Data moves between devices by JAX's collectives and lax.ppermute only.
A program may use at most 192 MiB of HBM per device.

v0:
```python
import jax
import jax.numpy as jnp
from jax import lax
from jax.sharding import PartitionSpec as P

HEADS = 16
KV_HEADS = 8
HEAD_DIM = 128
WINDOW = 1024
ADAM_STEP = 10


SOFT_CAP = 50.0
SCORE_SCALE = 1.0 / 12.0
LEARN_RATE = 0.01
BETA_ONE = 0.9
BETA_TWO = 0.95
EPSILON = 1e-08


def passed_along(block, axis, distance):
    devices = range(lax.axis_size(axis))
    route = [(i - distance, i) for i in devices if i - distance in devices]
    return lax.ppermute(block, axis, route)


def window_mask(query_start, key_start, query_count, key_count, seq_len):
    query_pos = query_start + lax.iota(jnp.int32, query_count)
    key_pos = key_start + lax.iota(jnp.int32, key_count)
    distance = query_pos[:, None] - key_pos[None, :]
    visible = (
        (key_pos[None, :] >= 0)
        & (query_pos[:, None] < seq_len)
        & (distance >= 0)
        & (distance < WINDOW)
    )
    return (visible, query_pos < seq_len)


def capped_weights(query_heads, key_heads, visible):
    raw_scores = (
        jnp.einsum("agrd,bgd->grab", query_heads, key_heads, preferred_element_type=jnp.float32)
        * SCORE_SCALE
    )
    capped = SOFT_CAP * jnp.tanh(raw_scores / SOFT_CAP)
    weights = jnp.where(visible[None, None], jnp.exp(capped), 0.0).astype(jnp.bfloat16)
    return (capped, weights)


def score_terms(grad_heads, value_heads, capped, weights, totals, deltas):
    normed = weights.astype(jnp.float32) / totals[..., None]
    prob_grad = jnp.einsum(
        "agrd,bgd->grab", grad_heads, value_heads, preferred_element_type=jnp.float32
    )
    score_grad = (
        normed * (prob_grad - deltas[..., None]) * (1.0 - (capped / SOFT_CAP) ** 2)
    ).astype(jnp.bfloat16)
    return (normed.astype(jnp.bfloat16), score_grad)


def on_device(
    query_rows, key_rows, value_rows, out_grad, gate_grads, first_moment, second_moment, master_rows
):
    tokens = query_rows.shape[1]
    group_size = HEADS // KV_HEADS
    ctx_count = lax.axis_size("ctx")
    ctx_index = lax.axis_index("ctx")
    reach = (WINDOW - 1) // tokens + 1
    seq_len = tokens * ctx_count
    query_heads = query_rows[0].reshape(tokens, KV_HEADS, group_size, HEAD_DIM)
    grad_heads = out_grad[0].reshape(tokens, KV_HEADS, group_size, HEAD_DIM)
    key_heads = key_rows[0].reshape(tokens, KV_HEADS, HEAD_DIM)
    value_heads = value_rows[0].reshape(tokens, KV_HEADS, HEAD_DIM)
    earlier = []
    for offset in range(reach, 0, -1):
        earlier.append(passed_along((key_heads, value_heads), "ctx", offset))
    key_list = []
    value_list = []
    for shifted in earlier:
        key_list.append(shifted[0])
        value_list.append(shifted[1])
    key_all = jnp.concatenate(key_list + [key_heads], axis=0)
    value_all = jnp.concatenate(value_list + [value_heads], axis=0)
    visible, query_live = window_mask(
        ctx_index * tokens, (ctx_index - reach) * tokens, tokens, (reach + 1) * tokens, seq_len
    )
    capped, weights = capped_weights(query_heads, key_all, visible)
    totals = jnp.sum(weights.astype(jnp.float32), axis=3)
    weighted = jnp.einsum("grab,bgd->agrd", weights, value_all, preferred_element_type=jnp.float32)
    attended = (weighted / jnp.transpose(totals, (2, 0, 1))[..., None]).astype(jnp.bfloat16)
    deltas = jnp.transpose(
        jnp.sum(grad_heads.astype(jnp.float32) * attended.astype(jnp.float32), axis=3), (1, 2, 0)
    )
    rounded, score_grad = score_terms(grad_heads, value_all, capped, weights, totals, deltas)
    query_grad = (
        jnp.einsum("grab,bgd->agrd", score_grad, key_all, preferred_element_type=jnp.float32)
        * SCORE_SCALE
    ).astype(jnp.bfloat16)
    key_part = jnp.einsum(
        "grab,agrd->bgd", score_grad, query_heads, preferred_element_type=jnp.float32
    )
    value_part = jnp.einsum(
        "grab,agrd->bgd", rounded, grad_heads, preferred_element_type=jnp.float32
    )
    key_acc = key_part[reach * tokens :]
    value_acc = value_part[reach * tokens :]
    for offset in range(1, reach + 1):
        first_row = (reach - offset) * tokens
        returned = passed_along(
            (key_part[first_row : first_row + tokens], value_part[first_row : first_row + tokens]),
            "ctx",
            -offset,
        )
        key_acc = key_acc + returned[0]
        value_acc = value_acc + returned[1]
    query_out = query_grad.reshape(1, tokens, HEADS * HEAD_DIM)
    key_out = (key_acc * SCORE_SCALE).astype(jnp.bfloat16).reshape(1, tokens, KV_HEADS * HEAD_DIM)
    value_out = value_acc.astype(jnp.bfloat16).reshape(1, tokens, KV_HEADS * HEAD_DIM)
    partial_value = gate_grads[0].astype(jnp.float32)
    summed = lax.psum_scatter(
        partial_value.astype(jnp.bfloat16), "dp", scatter_dimension=1, tiled=True
    ).astype(jnp.float32)
    new_first = BETA_ONE * first_moment + (1.0 - BETA_ONE) * summed
    new_second = BETA_TWO * second_moment + (1.0 - BETA_TWO) * summed * summed
    fix_one = 1.0 - BETA_ONE**ADAM_STEP
    fix_two = 1.0 - BETA_TWO**ADAM_STEP
    new_master = master_rows - LEARN_RATE * (new_first / fix_one) / (
        jnp.sqrt(new_second / fix_two) + EPSILON
    )
    gate_params = lax.all_gather(new_master.astype(jnp.bfloat16), "dp", axis=1, tiled=True)
    return (query_out, key_out, value_out, gate_params, new_first, new_second, new_master)


def solution(mesh):
    placed = (
        P("dp", "ctx", None),
        P("dp", "ctx", None),
        P("dp", "ctx", None),
        P("dp", "ctx", None),
        P("dp", "ctx", None),
        P("ctx", "dp"),
        P("ctx", "dp"),
        P("ctx", "dp"),
    )
    return jax.shard_map(
        on_device,
        mesh=mesh,
        in_specs=placed,
        out_specs=(
            P("dp", "ctx", None),
            P("dp", "ctx", None),
            P("dp", "ctx", None),
            P("ctx", None),
            P("ctx", "dp"),
            P("ctx", "dp"),
            P("ctx", "dp"),
        ),
        check_vma=False,
    )
```

profile of v0, /device:TPU:16, one launch (start us, length us, event | category | flops | bytes accessed | tf_op | source)
XLA Modules:
  0.0 334.5 jit_solution(3787062654881334468)
XLA Ops:
  7.2 0.0 reduce-scatter.4.cloned.1.call-start
  7.2 1.2 copy.54
  8.5 0.3 copy.55
  8.7 4.6 %collective-permute-start = (bf16[256,8,128]{2,0,1:T(8,128)(2,1)S(1)}, bf16[256,8,128]{2,0,1:T(8,128)(2,1)}, u32[]{:S(2)}, u32[]{:S(2)}) collective-permute-start(bf16[256,8,128]{2,0,1:T(8,128)(2,1)S(1)} %copy.55), channel_id=1, source_target_pairs={{0,4},{1,5},{2,6},{3,7},{4,8},{5,9},{6,10},{7,11},{8,12},{9,13},{1... | collective-permute-start | bytes 1572872 | tf_op jit(solution)/shard_map/ppermute | solution.py:24
  13.4 3.7 %collective-permute-start.1 = (bf16[256,8,128]{2,0,1:T(8,128)(2,1)S(1)}, bf16[256,8,128]{2,0,1:T(8,128)(2,1)}, u32[]{:S(2)}, u32[]{:S(2)}) collective-permute-start(bf16[256,8,128]{2,0,1:T(8,128)(2,1)S(1)} %copy.55), channel_id=1, source_target_pairs={{0,3},{1,4},{2,5},{3,6},{4,7},{5,8},{6,9},{7,10},{8,11},{9,12},{10... | collective-permute-start | bytes 1572872 | tf_op jit(solution)/shard_map/ppermute | solution.py:24
  17.1 4.0 %collective-permute-start.2 = (bf16[256,8,128]{2,0,1:T(8,128)(2,1)S(1)}, bf16[256,8,128]{2,0,1:T(8,128)(2,1)}, u32[]{:S(2)}, u32[]{:S(2)}) collective-permute-start(bf16[256,8,128]{2,0,1:T(8,128)(2,1)S(1)} %copy.55), channel_id=1, source_target_pairs={{0,2},{1,3},{2,4},{3,5},{4,6},{5,7},{6,8},{7,9},{8,10},{9,11},{10,... | collective-permute-start | bytes 1572872 | tf_op jit(solution)/shard_map/ppermute | solution.py:24
  21.1 2.9 collective-permute-start.3
  24.0 1.2 copy.61
  25.2 0.3 copy.62
  25.5 2.9 collective-permute-start.4
  28.4 2.6 copy.95
  31.1 0.0 reduce-scatter.4.cloned.1.call-update
  31.1 0.0 all-gather.3.cloned.1.call-start
  31.2 1.0 fusion.21
  32.2 1.5 copy.97
  33.7 2.3 copy.67
  35.9 3.5 %collective-permute-start.5 = (bf16[256,8,128]{2,0,1:T(8,128)(2,1)S(1)}, bf16[256,8,128]{2,0,1:T(8,128)(2,1)S(1)}, u32[]{:S(2)}, u32[]{:S(2)}) collective-permute-start(bf16[256,8,128]{2,0,1:T(8,128)(2,1)S(1)} %copy.62), channel_id=1, source_target_pairs={{0,3},{1,4},{2,5},{3,6},{4,7},{5,8},{6,9},{7,10},{8,11},{9,12},{10... | collective-permute-start | bytes 1572872 | tf_op jit(solution)/shard_map/ppermute | solution.py:24
  39.4 1.1 constant_dynamic-update-slice_fusion.4
  40.5 5.1 %collective-permute-start.6 = (bf16[256,8,128]{2,0,1:T(8,128)(2,1)S(1)}, bf16[256,8,128]{2,0,1:T(8,128)(2,1)S(1)}, u32[]{:S(2)}, u32[]{:S(2)}) collective-permute-start(bf16[256,8,128]{2,0,1:T(8,128)(2,1)S(1)} %copy.62), channel_id=1, source_target_pairs={{0,2},{1,3},{2,4},{3,5},{4,6},{5,7},{6,8},{7,9},{8,10},{9,11},{10,... | collective-permute-start | bytes 1572872 | tf_op jit(solution)/shard_map/ppermute | solution.py:24
  45.6 1.2 constant_dynamic-update-slice_fusion.3
  46.8 0.6 collective-permute-done.2
  47.3 3.2 collective-permute-start.7
  50.5 1.1 constant_dynamic-update-slice_fusion.2
  51.6 1.1 constant_dynamic-update-slice_fusion.1
  52.8 0.1 constant_dynamic-update-slice_fusion
  52.9 0.0 copy-start.3
  52.9 10.5 %convert_reduce_fusion = (f32[8,2,256]{2,1,0:T(2,128)S(1)}, f32[8,1280,256,2]{2,1,3,0:T(8,128)}) fusion(pred[256,1280]{0,1:T(8,128)(4,1)S(1)} %fusion.21, bf16[256,8,2,128]{0,3,2,1:T(8,128)(2,1)S(1)} %bitcast.96, bf16[1280,8,128]{2,0,1:T(8,128)(2,1)S(1)} %constant_dynamic-update-slice_fusion), kind=kOutput, calls=%fused_computation.1 | convolution fusion | flops 1373630464 | bytes 24985600 | tf_op jit(solution)/shard_map/agrd,bgd->grab/dot_general | solution.py:42
  63.4 9.8 %fusion.6 = f32[1280,8,128]{0,2,1:T(8,128)S(1)} fusion(bf16[256,8,2,128]{0,3,2,1:T(8,128)(2,1)S(1)} %bitcast.105, f32[8,2,256]{2,1,0:T(2,128)S(1)} %get-tuple-element.40, f32[8,1280,256,2]{2,1,3,0:T(8,128)} %get-tuple-element.41, pred[256,1280]{0,1:T(8,128)(4,1)S(1)} %fusion.21), kind=kOutput, calls=%fused_computation.12 | convolution fusion | flops 1373634560 | bytes 27607040 | tf_op jit(solution)/shard_map/grab,agrd->bgd/dot_general | solution.py:102
  73.1 2.3 fusion.39
  75.4 2.6 collective-permute-start.12
  78.1 1.9 collective-permute-start.13
  80.1 5.5 %collective-permute-done.5 = bf16[256,8,128]{2,0,1:T(8,128)(2,1)S(1)} collective-permute-done((bf16[256,8,128]{2,0,1:T(8,128)(2,1)S(1)}, bf16[256,8,128]{2,0,1:T(8,128)(2,1)S(1)}, u32[]{:S(2)}, u32[]{:S(2)}) %collective-permute-start.5) | collective-permute-done | bytes 524320 | tf_op jit(solution)/shard_map/ppermute | solution.py:24
  85.6 1.3 collective-permute-start.14
  86.9 0.1 constant_dynamic-update-slice_fusion.8
  87.0 11.9 %collective-permute-done.6 = bf16[256,8,128]{2,0,1:T(8,128)(2,1)S(1)} collective-permute-done((bf16[256,8,128]{2,0,1:T(8,128)(2,1)S(1)}, bf16[256,8,128]{2,0,1:T(8,128)(2,1)S(1)}, u32[]{:S(2)}, u32[]{:S(2)}) %collective-permute-start.6) | collective-permute-done | bytes 524320 | tf_op jit(solution)/shard_map/ppermute | solution.py:24
  98.9 1.5 collective-permute-start.15
  100.3 0.1 constant_dynamic-update-slice_fusion.7
  100.4 0.1 constant_dynamic-update-slice_fusion.6
  100.5 0.1 constant_dynamic-update-slice_fusion.5
  100.6 10.6 %multiply_reduce_fusion = f32[256,8,2]{0,2,1:T(2,128)S(1)} fusion(bf16[256,8,2,128]{0,3,2,1:T(8,128)(2,1)S(1)} %bitcast.106, f32[256,8,2]{0,2,1:T(2,128)S(1)} %bitcast.109, bf16[1280,8,128]{2,0,1:T(8,128)(2,1)S(1)} %constant_dynamic-update-slice_fusion.5, f32[8,1280,256,2]{2,1,3,0:T(8,128)} %get-tuple-element.41, pred[256,1280]{0,1:T(8,128)(4,1)S(1)} %fusion.21), kind=kOutput, calls=%fused_computation.22 | convolution fusion | flops 1361047552 | bytes 25001984 | tf_op jit(solution)/shard_map/grab,bgd->agrd/dot_general | solution.py:89
  111.2 0.0 copy-start.4
  111.2 0.0 copy-start.5
  111.2 15.7 %fusion = bf16[8,2,256,1280]{2,3,1,0:T(8,128)(2,1)} fusion(f32[8,1280,256,2]{2,1,3,0:T(8,128)} %get-tuple-element.41, bf16[256,8,2,128]{0,3,2,1:T(8,128)(2,1)S(1)} %bitcast.107, f32[8,2,256]{2,1,0:T(2,128)S(1)} %bitcast.110, f32[8,2,256]{2,1,0:T(2,128)S(1)} %get-tuple-element.40, bf16[1280,8,128]{2,0,1:T(8,128)(2,1)S(1)} %constant_dynamic-update-slice_fusion.5, ...), kind=kOutput, calls=%fused_computation.3 | convolution fusion | flops 1399848960 | bytes 35487744 | tf_op jit(solution)/shard_map/agrd,bgd->grab/dot_general | solution.py:52
  126.9 1.2 copy.96
  128.2 2.9 convert_bitcast_fusion
  131.1 0.0 all-gather.3.cloned.1.call-update
  131.2 10.0 %convolution_bitcast_fusion = f32[1280,8,128]{0,2,1:T(8,128)} fusion(bf16[8,2,256,1280]{2,3,1,0:T(8,128)(2,1)} %fusion, bf16[256,8,2,128]{0,3,2,1:T(8,128)(2,1)S(1)} %bitcast.97), kind=kOutput, calls=%fused_computation.11 | convolution fusion | flops 1342177280 | bytes 16777216 | tf_op jit(solution)/shard_map/grab,agrd->bgd/dot_general | solution.py:99
  141.1 4.6 %fusion.40 = (f32[256,8,128]{0,2,1:T(8,128)}, f32[256,8,128]{0,2,1:T(8,128)}, f32[256,8,128]{0,2,1:T(8,128)}, f32[256,8,128]{0,2,1:T(8,128)}) fusion(f32[1280,8,128]{0,2,1:T(8,128)} %convolution_bitcast_fusion), kind=kLoop, calls=%fused_computation.59 | loop fusion | bytes 8388608 | tf_op jit(solution)/shard_map/slice | solution.py:110
  145.7 1.4 collective-permute-start.10
  147.1 1.3 collective-permute-start.11
  148.4 21.2 %collective-permute-done.13 = f32[256,8,128]{0,2,1:T(8,128)} collective-permute-done((f32[256,8,128]{0,2,1:T(8,128)}, f32[256,8,128]{0,2,1:T(8,128)}, u32[]{:S(2)}, u32[]{:S(2)}) %collective-permute-start.13) | collective-permute-done | bytes 1048608 | tf_op jit(solution)/shard_map/ppermute | solution.py:24
  169.6 1.9 collective-permute-start.8
  171.5 2.1 collective-permute-start.9
  173.7 1.7 multiply_convert_fusion
  175.4 1.4 copy.77
  176.9 2.8 fusion.25
  179.7 1.0 copy.79
  180.7 50.9 %collective-permute-done.10 = f32[256,8,128]{0,2,1:T(8,128)} collective-permute-done((f32[256,8,128]{0,2,1:T(8,128)}, f32[256,8,128]{0,2,1:T(8,128)}, u32[]{:S(2)}, u32[]{:S(2)}) %collective-permute-start.10) | collective-permute-done | bytes 1048608 | tf_op jit(solution)/shard_map/ppermute | solution.py:24
  231.6 0.5 collective-permute-done.11
  232.1 87.5 %collective-permute-done.9 = f32[256,8,128]{0,2,1:T(8,128)} collective-permute-done((f32[256,8,128]{0,2,1:T(8,128)}, f32[256,8,128]{0,2,1:T(8,128)}, u32[]{:S(2)}, u32[]{:S(2)}) %collective-permute-start.9) | collective-permute-done | bytes 1048608 | tf_op jit(solution)/shard_map/ppermute | solution.py:24
  319.7 2.9 fusion.30
  322.5 1.0 copy.78
  323.5 2.1 copy.76
  325.7 2.0 reshape.104
  (32 shorter events, 0.1 us)
Async XLA Ops:
  7.2 119.8 %reduce-scatter.4.cloned.1.call-start = ((), (), s32[]{:S(2)}) async-start(), calls=%async_computation.2 | async-start | bytes 2211840
  8.7 27.2 %collective-permute-start = (bf16[256,8,128]{2,0,1:T(8,128)(2,1)S(1)}, bf16[256,8,128]{2,0,1:T(8,128)(2,1)}, u32[]{:S(2)}, u32[]{:S(2)}) collective-permute-start(bf16[256,8,128]{2,0,1:T(8,128)(2,1)S(1)} %copy.55), channel_id=1, source_target_pairs={{0,4},{1,5},{2,6},{3,7},{4,8},{5,9},{6,10},{7,11},{8,12},{9,13},{1... | collective-permute-start | bytes 1572872 | tf_op jit(solution)/shard_map/ppermute | solution.py:24
  13.4 27.1 %collective-permute-start.1 = (bf16[256,8,128]{2,0,1:T(8,128)(2,1)S(1)}, bf16[256,8,128]{2,0,1:T(8,128)(2,1)}, u32[]{:S(2)}, u32[]{:S(2)}) collective-permute-start(bf16[256,8,128]{2,0,1:T(8,128)(2,1)S(1)} %copy.55), channel_id=1, source_target_pairs={{0,3},{1,4},{2,5},{3,6},{4,7},{5,8},{6,9},{7,10},{8,11},{9,12},{10... | collective-permute-start | bytes 1572872 | tf_op jit(solution)/shard_map/ppermute | solution.py:24
  17.1 30.2 %collective-permute-start.2 = (bf16[256,8,128]{2,0,1:T(8,128)(2,1)S(1)}, bf16[256,8,128]{2,0,1:T(8,128)(2,1)}, u32[]{:S(2)}, u32[]{:S(2)}) collective-permute-start(bf16[256,8,128]{2,0,1:T(8,128)(2,1)S(1)} %copy.55), channel_id=1, source_target_pairs={{0,2},{1,3},{2,4},{3,5},{4,6},{5,7},{6,8},{7,9},{8,10},{9,11},{10,... | collective-permute-start | bytes 1572872 | tf_op jit(solution)/shard_map/ppermute | solution.py:24
  21.1 30.5 %collective-permute-start.3 = (bf16[256,8,128]{2,0,1:T(8,128)(2,1)S(1)}, bf16[256,8,128]{2,0,1:T(8,128)(2,1)}, u32[]{:S(2)}, u32[]{:S(2)}) collective-permute-start(bf16[256,8,128]{2,0,1:T(8,128)(2,1)S(1)} %copy.55), channel_id=1, source_target_pairs={{0,1},{1,2},{2,3},{3,4},{4,5},{5,6},{6,7},{7,8},{8,9},{9,10},{10,1... | collective-permute-start | bytes 1572872 | tf_op jit(solution)/shard_map/ppermute | solution.py:24
  25.5 52.6 %collective-permute-start.4 = (bf16[256,8,128]{2,0,1:T(8,128)(2,1)S(1)}, bf16[256,8,128]{2,0,1:T(8,128)(2,1)S(1)}, u32[]{:S(2)}, u32[]{:S(2)}) collective-permute-start(bf16[256,8,128]{2,0,1:T(8,128)(2,1)S(1)} %copy.62), channel_id=1, source_target_pairs={{0,4},{1,5},{2,6},{3,7},{4,8},{5,9},{6,10},{7,11},{8,12},{9,13},{1... | collective-permute-start | bytes 1572872 | tf_op jit(solution)/shard_map/ppermute | solution.py:24
  31.1 292.4 %all-gather.3.cloned.1.call-start = ((), (), s32[]{:S(2)}) async-start(), calls=%async_computation.1 | async-start | bytes 1843200 | tf_op jit(solution)/shard_map/all_gather | solution.py:130
  35.9 49.7 %collective-permute-start.5 = (bf16[256,8,128]{2,0,1:T(8,128)(2,1)S(1)}, bf16[256,8,128]{2,0,1:T(8,128)(2,1)S(1)}, u32[]{:S(2)}, u32[]{:S(2)}) collective-permute-start(bf16[256,8,128]{2,0,1:T(8,128)(2,1)S(1)} %copy.62), channel_id=1, source_target_pairs={{0,3},{1,4},{2,5},{3,6},{4,7},{5,8},{6,9},{7,10},{8,11},{9,12},{10... | collective-permute-start | bytes 1572872 | tf_op jit(solution)/shard_map/ppermute | solution.py:24
  40.5 58.4 %collective-permute-start.6 = (bf16[256,8,128]{2,0,1:T(8,128)(2,1)S(1)}, bf16[256,8,128]{2,0,1:T(8,128)(2,1)S(1)}, u32[]{:S(2)}, u32[]{:S(2)}) collective-permute-start(bf16[256,8,128]{2,0,1:T(8,128)(2,1)S(1)} %copy.62), channel_id=1, source_target_pairs={{0,2},{1,3},{2,4},{3,5},{4,6},{5,7},{6,8},{7,9},{8,10},{9,11},{10,... | collective-permute-start | bytes 1572872 | tf_op jit(solution)/shard_map/ppermute | solution.py:24
  47.3 53.1 %collective-permute-start.7 = (bf16[256,8,128]{2,0,1:T(8,128)(2,1)S(1)}, bf16[256,8,128]{2,0,1:T(8,128)(2,1)S(1)}, u32[]{:S(2)}, u32[]{:S(2)}) collective-permute-start(bf16[256,8,128]{2,0,1:T(8,128)(2,1)S(1)} %copy.62), channel_id=1, source_target_pairs={{0,1},{1,2},{2,3},{3,4},{4,5},{5,6},{6,7},{7,8},{8,9},{9,10},{10,1... | collective-permute-start | bytes 1572872 | tf_op jit(solution)/shard_map/ppermute | solution.py:24
  52.8 10.5 %copy-start.1 = (bf16[1280,8,128]{2,0,1:T(8,128)(2,1)}, bf16[1280,8,128]{2,0,1:T(8,128)(2,1)S(1)}, u32[]{:S(2)}) copy-start(bf16[1280,8,128]{2,0,1:T(8,128)(2,1)S(1)} %constant_dynamic-update-slice_fusion) | copy-start | bytes 7864324
  52.9 10.5 %copy-start.3 = (bf16[1,256,2048]{1,2,0:T(8,128)(2,1)S(1)}, bf16[1,256,2048]{1,2,0:T(8,128)(2,1)}, u32[]{:S(2)}) copy-start(bf16[1,256,2048]{1,2,0:T(8,128)(2,1)} %copy.67) | copy-start | bytes 3145732
  73.1 13.8 %copy-start = (f32[1280,8,128]{0,2,1:T(8,128)}, f32[1280,8,128]{0,2,1:T(8,128)S(1)}, u32[]{:S(2)}) copy-start(f32[1280,8,128]{0,2,1:T(8,128)S(1)} %fusion.6) | copy-start | bytes 15728644
  75.4 71.7 %collective-permute-start.12 = (f32[256,8,128]{0,2,1:T(8,128)}, f32[256,8,128]{0,2,1:T(8,128)}, u32[]{:S(2)}, u32[]{:S(2)}) collective-permute-start(f32[256,8,128]{0,2,1:T(8,128)} %get-tuple-element.32), channel_id=1, source_target_pairs={{1,0},{2,1},{3,2},{4,3},{5,4},{6,5},{7,6},{8,7},{9,8},{10,9},{11,1... | collective-permute-start | bytes 3145736 | tf_op jit(solution)/shard_map/ppermute | solution.py:24
  78.1 91.5 %collective-permute-start.13 = (f32[256,8,128]{0,2,1:T(8,128)}, f32[256,8,128]{0,2,1:T(8,128)}, u32[]{:S(2)}, u32[]{:S(2)}) collective-permute-start(f32[256,8,128]{0,2,1:T(8,128)} %get-tuple-element.35), channel_id=1, source_target_pairs={{2,0},{3,1},{4,2},{5,3},{6,4},{7,5},{8,6},{9,7},{10,8},{11,9},{12,... | collective-permute-start | bytes 3145736 | tf_op jit(solution)/shard_map/ppermute | solution.py:24
  85.6 85.9 %collective-permute-start.14 = (f32[256,8,128]{0,2,1:T(8,128)}, f32[256,8,128]{0,2,1:T(8,128)}, u32[]{:S(2)}, u32[]{:S(2)}) collective-permute-start(f32[256,8,128]{0,2,1:T(8,128)} %get-tuple-element.34), channel_id=1, source_target_pairs={{3,0},{4,1},{5,2},{6,3},{7,4},{8,5},{9,6},{10,7},{11,8},{12,9},{13... | collective-permute-start | bytes 3145736 | tf_op jit(solution)/shard_map/ppermute | solution.py:24
  98.9 78.0 %collective-permute-start.15 = (f32[256,8,128]{0,2,1:T(8,128)}, f32[256,8,128]{0,2,1:T(8,128)}, u32[]{:S(2)}, u32[]{:S(2)}) collective-permute-start(f32[256,8,128]{0,2,1:T(8,128)} %get-tuple-element.33), channel_id=1, source_target_pairs={{4,0},{5,1},{6,2},{7,3},{8,4},{9,5},{10,6},{11,7},{12,8},{13,9},{1... | collective-permute-start | bytes 3145736 | tf_op jit(solution)/shard_map/ppermute | solution.py:24
  111.2 17.0 %copy-start.4 = (f32[288,576]{1,0:T(8,128)S(1)}, f32[288,576]{1,0:T(8,128)}, u32[]{:S(2)}) copy-start(f32[288,576]{1,0:T(8,128)} %param.15) | copy-start | bytes 1990660
  111.2 17.0 %copy-start.5 = (f32[288,576]{1,0:T(8,128)S(1)}, f32[288,576]{1,0:T(8,128)}, u32[]{:S(2)}) copy-start(f32[288,576]{1,0:T(8,128)} %param.13) | copy-start | bytes 1990660
  131.1 42.5 %slice-start = ((s8[10485760]{0:T(1024)(128)(4,1)}), s8[4194304]{0:T(1024)(128)(4,1)S(1)}, s32[]{:S(2)}) async-start(s8[10485760]{0:T(1024)(128)(4,1)} %bitcast.93), calls=%async_computation.3 | async-start | bytes 8388608
  131.1 42.5 %slice-start.1 = ((s8[10485760]{0:T(1024)(128)(4,1)}), s8[2097152]{0:T(1024)(128)(4,1)S(1)}, s32[]{:S(2)}) async-start(s8[10485760]{0:T(1024)(128)(4,1)} %bitcast.93), calls=%async_computation.4 | async-start | bytes 4194304
  141.1 32.6 %slice-start.2 = ((s8[10485760]{0:T(1024)(128)(4,1)}), s8[4194304]{0:T(1024)(128)(4,1)S(1)}, s32[]{:S(2)}) async-start(s8[10485760]{0:T(1024)(128)(4,1)} %bitcast.93), calls=%async_computation.5 | async-start | bytes 8388608
  141.1 32.6 %copy-start.2 = (bf16[1280,8,128]{2,0,1:T(8,128)(2,1)S(1)}, bf16[1280,8,128]{2,0,1:T(8,128)(2,1)}, u32[]{:S(2)}) copy-start(bf16[1280,8,128]{2,0,1:T(8,128)(2,1)} %copy-done.1) | copy-start | bytes 7864324
  145.7 85.9 %collective-permute-start.10 = (f32[256,8,128]{0,2,1:T(8,128)}, f32[256,8,128]{0,2,1:T(8,128)}, u32[]{:S(2)}, u32[]{:S(2)}) collective-permute-start(f32[256,8,128]{0,2,1:T(8,128)} %get-tuple-element.38), channel_id=1, source_target_pairs={{3,0},{4,1},{5,2},{6,3},{7,4},{8,5},{9,6},{10,7},{11,8},{12,9},{13... | collective-permute-start | bytes 3145736 | tf_op jit(solution)/shard_map/ppermute | solution.py:24
  147.1 85.0 %collective-permute-start.11 = (f32[256,8,128]{0,2,1:T(8,128)}, f32[256,8,128]{0,2,1:T(8,128)}, u32[]{:S(2)}, u32[]{:S(2)}) collective-permute-start(f32[256,8,128]{0,2,1:T(8,128)} %get-tuple-element.37), channel_id=1, source_target_pairs={{4,0},{5,1},{6,2},{7,3},{8,4},{9,5},{10,6},{11,7},{12,8},{13,9},{1... | collective-permute-start | bytes 3145736 | tf_op jit(solution)/shard_map/ppermute | solution.py:24
  169.6 62.5 %collective-permute-start.8 = (f32[256,8,128]{0,2,1:T(8,128)}, f32[256,8,128]{0,2,1:T(8,128)}, u32[]{:S(2)}, u32[]{:S(2)}) collective-permute-start(f32[256,8,128]{0,2,1:T(8,128)} %get-tuple-element.36), channel_id=1, source_target_pairs={{1,0},{2,1},{3,2},{4,3},{5,4},{6,5},{7,6},{8,7},{9,8},{10,9},{11,1... | collective-permute-start | bytes 3145736 | tf_op jit(solution)/shard_map/ppermute | solution.py:24
  171.5 148.2 %collective-permute-start.9 = (f32[256,8,128]{0,2,1:T(8,128)}, f32[256,8,128]{0,2,1:T(8,128)}, u32[]{:S(2)}, u32[]{:S(2)}) collective-permute-start(f32[256,8,128]{0,2,1:T(8,128)} %get-tuple-element.39), channel_id=1, source_target_pairs={{2,0},{3,1},{4,2},{5,3},{6,4},{7,5},{8,6},{9,7},{10,8},{11,9},{12,... | collective-permute-start | bytes 3145736 | tf_op jit(solution)/shard_map/ppermute | solution.py:24
Sparse Core Ops, SparseCore 0:
  31.2 65.2 reduce-scatter.3
  131.3 86.3 all-gather.2
where the time goes:
time: 336 us; the launch traced here: 335 us
  waiting for transfers between devices  178 us (53%)
  matrix products  58.3 us (17%)
  starting transfers between devices  44 us (13%)
  local copies, waits for them, and re-layouts  29.9 us (9%)
  between operations  14.5 us (4%)
  other arithmetic  9.6 us (3%)
    ppermute x16, waiting for transfers between devices, passed_along(): return lax.ppermute(block, axis, route)  178 us
    ppermute x16, starting transfers between devices, passed_along(): return lax.ppermute(block, axis, route)  43.9 us
    unnamed x35, local copies, waits for them, and re-layouts  18.8 us
    dot_general x1, matrix products, score_terms(): jnp.einsum('agrd,bgd->grab', grad_heads, value_heads, preferred_element_t...  15.7 us
    dot_general x1, matrix products, on_device(): jnp.einsum('grab,bgd->agrd', weights, value_all, preferred_element_type=j...  10.6 us
    dot_general x1, matrix products, capped_weights(): jnp.einsum('agrd,bgd->grab', query_heads, key_heads, preferred_element_ty...  10.5 us
    dot_general x1, matrix products, on_device(): jnp.einsum('grab,agrd->bgd', score_grad, query_heads, preferred_element_t...  9.96 us
    dot_general x1, matrix products, on_device(): jnp.einsum('grab,agrd->bgd', rounded, grad_heads, preferred_element_type=...  9.75 us
  transfers between devices with their start and end apart: 18, of which 7 were waited for; matrix products, arithmetic and copies ran while one was open for 28% of the time, Pallas kernels for 0%

commit v1 on v0

--- a/solution.py
+++ b/solution.py
@@ -71,14 +71,13 @@
     grad_heads = out_grad[0].reshape(tokens, KV_HEADS, group_size, HEAD_DIM)
     key_heads = key_rows[0].reshape(tokens, KV_HEADS, HEAD_DIM)
     value_heads = value_rows[0].reshape(tokens, KV_HEADS, HEAD_DIM)
-    earlier = []
-    for offset in range(reach, 0, -1):
-        earlier.append(passed_along((key_heads, value_heads), "ctx", offset))
+    packed = jnp.concatenate([key_heads, value_heads], axis=2)
     key_list = []
     value_list = []
-    for shifted in earlier:
-        key_list.append(shifted[0])
-        value_list.append(shifted[1])
+    for offset in range(reach, 0, -1):
+        shifted = passed_along(packed, "ctx", offset)
+        key_list.append(shifted[:, :, :HEAD_DIM])
+        value_list.append(shifted[:, :, HEAD_DIM:])
     key_all = jnp.concatenate(key_list + [key_heads], axis=0)
     value_all = jnp.concatenate(value_list + [value_heads], axis=0)
     visible, query_live = window_mask(
@@ -106,13 +105,13 @@
     value_acc = value_part[reach * tokens :]
     for offset in range(1, reach + 1):
         first_row = (reach - offset) * tokens
-        returned = passed_along(
-            (key_part[first_row : first_row + tokens], value_part[first_row : first_row + tokens]),
-            "ctx",
-            -offset,
-        )
-        key_acc = key_acc + returned[0]
-        value_acc = value_acc + returned[1]
+        outgoing = jnp.concatenate(
+            [key_part[first_row : first_row + tokens], value_part[first_row : first_row + tokens]],
+            axis=2,
+        ).astype(jnp.bfloat16)
+        returned = passed_along(outgoing, "ctx", -offset).astype(jnp.float32)
+        key_acc = key_acc + returned[:, :, :HEAD_DIM]
+        value_acc = value_acc + returned[:, :, HEAD_DIM:]
     query_out = query_grad.reshape(1, tokens, HEADS * HEAD_DIM)
     key_out = (key_acc * SCORE_SCALE).astype(jnp.bfloat16).reshape(1, tokens, KV_HEADS * HEAD_DIM)
     value_out = value_acc.astype(jnp.bfloat16).reshape(1, tokens, KV_HEADS * HEAD_DIM)

time: 336 us -> 328 us (0.976)
  the two profiles are of different devices: /device:TPU:16 before, /device:TPU:248 now
where the time goes in v1:
time: 328 us; the launch traced here: 327 us
  waiting for transfers between devices  178 us (54%)
  matrix products  64.3 us (20%)
  starting transfers between devices  26.3 us (8%)
  local copies, waits for them, and re-layouts  24.6 us (8%)
  other arithmetic  19.1 us (6%)
  between operations  14.3 us (4%)
    ppermute x8, waiting for transfers between devices, passed_along(): return lax.ppermute(block, axis, route)  178 us
    ppermute x8, starting transfers between devices, passed_along(): return lax.ppermute(block, axis, route)  26.2 us
    unnamed x27, local copies, waits for them, and re-layouts  17.8 us
    dot_general x1, matrix products, score_terms(): jnp.einsum('agrd,bgd->grab', grad_heads, value_heads, preferred_element_t...  15.6 us
    dot_general x1, matrix products, on_device(): jnp.einsum('grab,agrd->bgd', rounded, grad_heads, preferred_element_type=...  12.3 us
    dot_general x1, matrix products, on_device(): jnp.einsum('grab,bgd->agrd', weights, value_all, preferred_element_type=j...  10.6 us
    dot_general x1, matrix products, capped_weights(): jnp.einsum('agrd,bgd->grab', query_heads, key_heads, preferred_element_ty...  10.2 us
    dot_general x1, matrix products, on_device(): jnp.einsum('grab,agrd->bgd', score_grad, query_heads, preferred_element_t...  9.83 us
  transfers between devices with their start and end apart: 10, of which 8 were waited for; matrix products, arithmetic and copies ran while one was open for 29% of the time, Pallas kernels for 0%

profile of v1, /device:TPU:248, one launch (start us, length us, event | category | flops | bytes accessed | tf_op | source)
XLA Modules:
  0.0 326.7 jit_solution(11181684467433830430)
XLA Ops:
  7.2 0.0 reduce-scatter.4.cloned.1.call-start
  7.2 1.2 copy.49
  8.5 0.0 copy-start.4
  8.5 0.3 copy.51
  8.7 1.4 copy.48
  10.1 0.3 copy.50
  10.4 1.1 pad_maximum_fusion
  11.5 4.7 %collective-permute-start = (bf16[256,8,256]{2,0,1:T(8,128)(2,1)}, bf16[256,8,256]{2,0,1:T(8,128)(2,1)}, u32[]{:S(2)}, u32[]{:S(2)}) collective-permute-start(bf16[256,8,256]{2,0,1:T(8,128)(2,1)} %pad_maximum_fusion), channel_id=1, source_target_pairs={{0,4},{1,5},{2,6},{3,7},{4,8},{5,9},{6,10},{7,11},{8,12},{9,13},{1... | collective-permute-start | bytes 3145736 | tf_op jit(solution)/shard_map/ppermute | solution.py:24
  16.2 3.1 collective-permute-start.1
  19.3 3.3 %collective-permute-start.2 = (bf16[256,8,256]{2,0,1:T(8,128)(2,1)}, bf16[256,8,256]{2,0,1:T(8,128)(2,1)}, u32[]{:S(2)}, u32[]{:S(2)}) collective-permute-start(bf16[256,8,256]{2,0,1:T(8,128)(2,1)} %pad_maximum_fusion), channel_id=1, source_target_pairs={{0,2},{1,3},{2,4},{3,5},{4,6},{5,7},{6,8},{7,9},{8,10},{9,11},{10,... | collective-permute-start | bytes 3145736 | tf_op jit(solution)/shard_map/ppermute | solution.py:24
  22.6 4.1 %collective-permute-start.3 = (bf16[256,8,256]{2,0,1:T(8,128)(2,1)}, bf16[256,8,256]{2,0,1:T(8,128)(2,1)}, u32[]{:S(2)}, u32[]{:S(2)}) collective-permute-start(bf16[256,8,256]{2,0,1:T(8,128)(2,1)} %pad_maximum_fusion), channel_id=1, source_target_pairs={{0,1},{1,2},{2,3},{3,4},{4,5},{5,6},{6,7},{7,8},{8,9},{9,10},{10,1... | collective-permute-start | bytes 3145736 | tf_op jit(solution)/shard_map/ppermute | solution.py:24
  26.7 0.0 copy-done.4
  26.8 1.7 copy.83
  28.4 0.0 reduce-scatter.4.cloned.1.call-update
  28.4 0.0 all-gather.3.cloned.1.call-start
  28.5 1.6 copy.85
  30.1 0.0 copy-done.5
  30.1 1.3 copy.55
  31.4 1.0 fusion.21
  32.4 7.7 %collective-permute-done = bf16[256,8,256]{2,0,1:T(8,128)(2,1)} collective-permute-done((bf16[256,8,256]{2,0,1:T(8,128)(2,1)}, bf16[256,8,256]{2,0,1:T(8,128)(2,1)}, u32[]{:S(2)}, u32[]{:S(2)}) %collective-permute-start) | collective-permute-done | bytes 1048608 | tf_op jit(solution)/shard_map/ppermute | solution.py:24
  40.1 1.4 slice_dynamic-update-slice_fusion.3
  41.5 28.8 %collective-permute-done.1 = bf16[256,8,256]{2,0,1:T(8,128)(2,1)} collective-permute-done((bf16[256,8,256]{2,0,1:T(8,128)(2,1)}, bf16[256,8,256]{2,0,1:T(8,128)(2,1)}, u32[]{:S(2)}, u32[]{:S(2)}) %collective-permute-start.1) | collective-permute-done | bytes 1048608 | tf_op jit(solution)/shard_map/ppermute | solution.py:24
  70.2 1.4 slice_dynamic-update-slice_fusion.2
  71.6 23.1 %collective-permute-done.2 = bf16[256,8,256]{2,0,1:T(8,128)(2,1)} collective-permute-done((bf16[256,8,256]{2,0,1:T(8,128)(2,1)}, bf16[256,8,256]{2,0,1:T(8,128)(2,1)}, u32[]{:S(2)}, u32[]{:S(2)}) %collective-permute-start.2) | collective-permute-done | bytes 1048608 | tf_op jit(solution)/shard_map/ppermute | solution.py:24
  94.8 1.4 slice_dynamic-update-slice_fusion.1
  96.1 30.4 %collective-permute-done.3 = bf16[256,8,256]{2,0,1:T(8,128)(2,1)} collective-permute-done((bf16[256,8,256]{2,0,1:T(8,128)(2,1)}, bf16[256,8,256]{2,0,1:T(8,128)(2,1)}, u32[]{:S(2)}, u32[]{:S(2)}) %collective-permute-start.3) | collective-permute-done | bytes 1048608 | tf_op jit(solution)/shard_map/ppermute | solution.py:24
  126.6 1.4 slice_dynamic-update-slice_fusion
  128.0 0.1 constant_dynamic-update-slice_fusion
  128.1 0.0 copy-start.6
  128.1 10.2 %convert_reduce_fusion = (f32[8,2,256]{2,1,0:T(2,128)S(1)}, f32[8,1280,256,2]{2,1,3,0:T(8,128)}) fusion(pred[256,1280]{0,1:T(8,128)(4,1)S(1)} %fusion.21, bf16[256,8,2,128]{0,3,2,1:T(8,128)(2,1)S(1)} %bitcast.96, bf16[1280,8,128]{2,0,1:T(8,128)(2,1)S(1)} %get-tuple-element.56), kind=kOutput, calls=%fused_computation.1 | convolution fusion | flops 1373630464 | bytes 24985600 | tf_op jit(solution)/shard_map/agrd,bgd->grab/dot_general | solution.py:42
  138.3 10.6 %multiply_reduce_fusion = f32[256,8,2]{0,2,1:T(2,128)S(1)} fusion(bf16[256,8,2,128]{0,3,2,1:T(8,128)(2,1)S(1)} %bitcast.105, f32[256,8,2]{0,2,1:T(2,128)S(1)} %bitcast.109, bf16[1280,8,128]{2,0,1:T(8,128)(2,1)S(1)} %get-tuple-element.57, f32[8,1280,256,2]{2,1,3,0:T(8,128)} %get-tuple-element.51, pred[256,1280]{0,1:T(8,128)(4,1)S(1)} %fusion.21), kind=kOutput, calls=%fused_computation.22 | convolution fusion | flops 1361047552 | bytes 25001984 | tf_op jit(solution)/shard_map/grab,bgd->agrd/dot_general | solution.py:88
  148.9 15.6 %fusion = bf16[8,2,256,1280]{2,3,1,0:T(8,128)(2,1)} fusion(f32[8,1280,256,2]{2,1,3,0:T(8,128)} %get-tuple-element.51, bf16[256,8,2,128]{0,3,2,1:T(8,128)(2,1)S(1)} %bitcast.106, f32[8,2,256]{2,1,0:T(2,128)S(1)} %bitcast.110, f32[8,2,256]{2,1,0:T(2,128)S(1)} %get-tuple-element.50, bf16[1280,8,128]{2,0,1:T(8,128)(2,1)S(1)} %get-tuple-element.57, ...), kind=kOutput, calls=%fused_computation.3 | convolution fusion | flops 1399848960 | bytes 35487744 | tf_op jit(solution)/shard_map/agrd,bgd->grab/dot_general | solution.py:52
  164.5 12.3 %fusion.35 = (bf16[1280,8,128]{0,2,1:T(8,128)(2,1)S(1)}, f32[1280,8,128]{0,2,1:T(8,128)}) fusion(bf16[256,8,2,128]{0,3,2,1:T(8,128)(2,1)S(1)} %bitcast.107, f32[8,2,256]{2,1,0:T(2,128)S(1)} %get-tuple-element.50, f32[8,1280,256,2]{2,1,3,0:T(8,128)} %get-tuple-element.51, pred[256,1280]{0,1:T(8,128)(4,1)S(1)} %fusion.21), kind=kOutput, calls=%fused_computation.65 | convolution fusion | flops 1374945280 | bytes 30228480 | tf_op jit(solution)/shard_map/grab,agrd->bgd/dot_general | solution.py:101
  176.8 1.2 fusion.34
  178.1 9.8 %fusion.36 = (bf16[1280,8,128]{0,2,1:T(8,128)(2,1)S(1)}, f32[1280,8,128]{0,2,1:T(8,128)}) fusion(bf16[8,2,256,1280]{2,3,1,0:T(8,128)(2,1)} %fusion, bf16[256,8,2,128]{0,3,2,1:T(8,128)(2,1)S(1)} %bitcast.97), kind=kOutput, calls=%fused_computation.66 | convolution fusion | flops 1343488000 | bytes 19398656 | tf_op jit(solution)/shard_map/grab,agrd->bgd/dot_general | solution.py:98
  187.9 1.2 fusion.33
  189.1 1.2 copy.84
  190.3 0.0 copy-start.2
  190.3 3.4 %convert_bitcast_fusion = (bf16[1,576,288]{1,2,0:T(8,128)(2,1)}, f32[288,576]{1,0:T(8,128)}, f32[288,576]{1,0:T(8,128)}, f32[288,576]{1,0:T(8,128)}) fusion(f32[288,576]{1,0:T(8,128)} %param.15, bf16[288,576]{1,0:T(8,128)(2,1)S(1)} %copy.84, f32[288,576]{1,0:T(8,128)} %param.13, f32[288,576]{1,0:T(8,128)} %param.14), kind=kLoop, calls=%fused_computation.56 | loop fusion | flops 2322432 | bytes 4644864
  193.7 0.0 all-gather.3.cloned.1.call-update
  193.8 2.3 pad_maximum_fusion.4
  196.0 1.9 collective-permute-start.7
  198.0 0.0 copy-done.2
  198.0 2.1 pad_maximum_fusion.3
  200.1 4.4 %collective-permute-start.6 = (bf16[256,8,256]{0,2,1:T(8,128)(2,1)}, bf16[256,8,256]{0,2,1:T(8,128)(2,1)}, u32[]{:S(2)}, u32[]{:S(2)}) collective-permute-start(bf16[256,8,256]{0,2,1:T(8,128)(2,1)} %pad_maximum_fusion.3), channel_id=1, source_target_pairs={{3,0},{4,1},{5,2},{6,3},{7,4},{8,5},{9,6},{10,7},{11,8},{12,9},{13... | collective-permute-start | bytes 3145736 | tf_op jit(solution)/shard_map/ppermute | solution.py:24
  204.6 1.0 pad_maximum_fusion.2
  205.6 1.9 collective-permute-start.5
  207.5 1.1 pad_maximum_fusion.1
  208.6 2.8 collective-permute-start.4
  211.4 5.7 %multiply_convert_fusion = bf16[8,128,2,256]{3,1,2,0:T(8,128)(2,1)S(1)} fusion(bf16[8,2,256,1280]{2,3,1,0:T(8,128)(2,1)} %fusion, bf16[1280,8,128]{2,0,1:T(8,128)(2,1)S(1)} %copy-done.1), kind=kOutput, calls=%fused_computation.21 | convolution fusion | flops 1343225856 | bytes 14155776 | tf_op jit(solution)/shard_map/grab,bgd->agrd/dot_general | solution.py:95
  217.2 1.4 copy.65
  218.6 22.2 %collective-permute-done.7 = bf16[256,8,256]{0,2,1:T(8,128)(2,1)} collective-permute-done((bf16[256,8,256]{0,2,1:T(8,128)(2,1)}, bf16[256,8,256]{0,2,1:T(8,128)(2,1)}, u32[]{:S(2)}, u32[]{:S(2)}) %collective-permute-start.7) | collective-permute-done | bytes 1048608 | tf_op jit(solution)/shard_map/ppermute | solution.py:24
  240.8 1.4 convert_element_type.70
  242.2 3.9 %collective-permute-done.6 = bf16[256,8,256]{0,2,1:T(8,128)(2,1)} collective-permute-done((bf16[256,8,256]{0,2,1:T(8,128)(2,1)}, bf16[256,8,256]{0,2,1:T(8,128)(2,1)}, u32[]{:S(2)}, u32[]{:S(2)}) %collective-permute-start.6) | collective-permute-done | bytes 1048608 | tf_op jit(solution)/shard_map/ppermute | solution.py:24
  246.2 1.4 convert_element_type.69
  247.6 10.5 %collective-permute-done.5 = bf16[256,8,256]{0,2,1:T(8,128)(2,1)} collective-permute-done((bf16[256,8,256]{0,2,1:T(8,128)(2,1)}, bf16[256,8,256]{0,2,1:T(8,128)(2,1)}, u32[]{:S(2)}, u32[]{:S(2)}) %collective-permute-start.5) | collective-permute-done | bytes 1048608 | tf_op jit(solution)/shard_map/ppermute | solution.py:24
  258.0 1.4 convert_element_type.68
  259.5 51.5 %collective-permute-done.4 = bf16[256,8,256]{0,2,1:T(8,128)(2,1)S(1)} collective-permute-done((bf16[256,8,256]{0,2,1:T(8,128)(2,1)}, bf16[256,8,256]{0,2,1:T(8,128)(2,1)S(1)}, u32[]{:S(2)}, u32[]{:S(2)}) %collective-permute-start.4) | collective-permute-done | bytes 1048608 | tf_op jit(solution)/shard_map/ppermute | solution.py:24
  311.0 0.2 convert_element_type.67
  311.2 2.6 fusion.22
  313.8 1.0 copy.66
  314.8 1.0 copy.67
  315.8 2.1 copy.64
  317.9 2.0 reshape.104
  (14 shorter events, 0.0 us)
Async XLA Ops:
  7.2 181.9 %reduce-scatter.4.cloned.1.call-start = ((), (), s32[]{:S(2)}) async-start(), calls=%async_computation.2 | async-start | bytes 2211840
  8.5 18.3 %copy-start.4 = (bf16[1,288,2304]{2,1,0:T(8,128)(2,1)S(1)}, bf16[1,288,2304]{2,1,0:T(8,128)(2,1)}, u32[]{:S(2)}) copy-start(bf16[1,288,2304]{2,1,0:T(8,128)(2,1)} %param.12) | copy-start | bytes 3981316
  11.5 28.6 %collective-permute-start = (bf16[256,8,256]{2,0,1:T(8,128)(2,1)}, bf16[256,8,256]{2,0,1:T(8,128)(2,1)}, u32[]{:S(2)}, u32[]{:S(2)}) collective-permute-start(bf16[256,8,256]{2,0,1:T(8,128)(2,1)} %pad_maximum_fusion), channel_id=1, source_target_pairs={{0,4},{1,5},{2,6},{3,7},{4,8},{5,9},{6,10},{7,11},{8,12},{9,13},{1... | collective-permute-start | bytes 3145736 | tf_op jit(solution)/shard_map/ppermute | solution.py:24
  16.2 54.0 %collective-permute-start.1 = (bf16[256,8,256]{2,0,1:T(8,128)(2,1)}, bf16[256,8,256]{2,0,1:T(8,128)(2,1)}, u32[]{:S(2)}, u32[]{:S(2)}) collective-permute-start(bf16[256,8,256]{2,0,1:T(8,128)(2,1)} %pad_maximum_fusion), channel_id=1, source_target_pairs={{0,3},{1,4},{2,5},{3,6},{4,7},{5,8},{6,9},{7,10},{8,11},{9,12},{10... | collective-permute-start | bytes 3145736 | tf_op jit(solution)/shard_map/ppermute | solution.py:24
  19.3 75.4 %collective-permute-start.2 = (bf16[256,8,256]{2,0,1:T(8,128)(2,1)}, bf16[256,8,256]{2,0,1:T(8,128)(2,1)}, u32[]{:S(2)}, u32[]{:S(2)}) collective-permute-start(bf16[256,8,256]{2,0,1:T(8,128)(2,1)} %pad_maximum_fusion), channel_id=1, source_target_pairs={{0,2},{1,3},{2,4},{3,5},{4,6},{5,7},{6,8},{7,9},{8,10},{9,11},{10,... | collective-permute-start | bytes 3145736 | tf_op jit(solution)/shard_map/ppermute | solution.py:24
  22.6 103.9 %collective-permute-start.3 = (bf16[256,8,256]{2,0,1:T(8,128)(2,1)}, bf16[256,8,256]{2,0,1:T(8,128)(2,1)}, u32[]{:S(2)}, u32[]{:S(2)}) collective-permute-start(bf16[256,8,256]{2,0,1:T(8,128)(2,1)} %pad_maximum_fusion), channel_id=1, source_target_pairs={{0,1},{1,2},{2,3},{3,4},{4,5},{5,6},{6,7},{7,8},{8,9},{9,10},{10,1... | collective-permute-start | bytes 3145736 | tf_op jit(solution)/shard_map/ppermute | solution.py:24
  28.4 1.6 copy-start.5
  28.4 287.3 %all-gather.3.cloned.1.call-start = ((), (), s32[]{:S(2)}) async-start(), calls=%async_computation.1 | async-start | bytes 1843200 | tf_op jit(solution)/shard_map/all_gather | solution.py:129
  128.1 10.2 %copy-start = (bf16[1280,8,128]{2,0,1:T(8,128)(2,1)}, bf16[1280,8,128]{2,0,1:T(8,128)(2,1)S(1)}, u32[]{:S(2)}) copy-start(bf16[1280,8,128]{2,0,1:T(8,128)(2,1)S(1)} %get-tuple-element.56) | copy-start | bytes 7864324
  128.1 10.2 %copy-start.6 = (bf16[1,256,2048]{1,2,0:T(8,128)(2,1)S(1)}, bf16[1,256,2048]{1,2,0:T(8,128)(2,1)}, u32[]{:S(2)}) copy-start(bf16[1,256,2048]{1,2,0:T(8,128)(2,1)} %copy.55) | copy-start | bytes 3145732
  190.3 7.6 %copy-start.2 = (bf16[256,8,128]{0,2,1:T(8,128)(2,1)S(1)}, bf16[256,8,128]{0,2,1:T(8,128)(2,1)}, u32[]{:S(2)}) copy-start(bf16[256,8,128]{0,2,1:T(8,128)(2,1)} %get-tuple-element.40) | copy-start | bytes 1572868
  193.7 10.8 %copy-start.3 = (bf16[256,8,128]{0,2,1:T(8,128)(2,1)S(1)}, bf16[256,8,128]{0,2,1:T(8,128)(2,1)}, u32[]{:S(2)}) copy-start(bf16[256,8,128]{0,2,1:T(8,128)(2,1)} %get-tuple-element.37) | copy-start | bytes 1572868
  196.0 44.8 %collective-permute-start.7 = (bf16[256,8,256]{0,2,1:T(8,128)(2,1)}, bf16[256,8,256]{0,2,1:T(8,128)(2,1)}, u32[]{:S(2)}, u32[]{:S(2)}) collective-permute-start(bf16[256,8,256]{0,2,1:T(8,128)(2,1)} %pad_maximum_fusion.4), channel_id=1, source_target_pairs={{4,0},{5,1},{6,2},{7,3},{8,4},{9,5},{10,6},{11,7},{12,8},{13,9},{1... | collective-permute-start | bytes 3145736 | tf_op jit(solution)/shard_map/ppermute | solution.py:24
  200.1 11.3 %copy-start.1 = (bf16[1280,8,128]{2,0,1:T(8,128)(2,1)S(1)}, bf16[1280,8,128]{2,0,1:T(8,128)(2,1)}, u32[]{:S(2)}) copy-start(bf16[1280,8,128]{2,0,1:T(8,128)(2,1)} %copy-done) | copy-start | bytes 7864324
  200.1 46.0 %collective-permute-start.6 = (bf16[256,8,256]{0,2,1:T(8,128)(2,1)}, bf16[256,8,256]{0,2,1:T(8,128)(2,1)}, u32[]{:S(2)}, u32[]{:S(2)}) collective-permute-start(bf16[256,8,256]{0,2,1:T(8,128)(2,1)} %pad_maximum_fusion.3), channel_id=1, source_target_pairs={{3,0},{4,1},{5,2},{6,3},{7,4},{8,5},{9,6},{10,7},{11,8},{12,9},{13... | collective-permute-start | bytes 3145736 | tf_op jit(solution)/shard_map/ppermute | solution.py:24
  205.6 52.4 %collective-permute-start.5 = (bf16[256,8,256]{0,2,1:T(8,128)(2,1)}, bf16[256,8,256]{0,2,1:T(8,128)(2,1)}, u32[]{:S(2)}, u32[]{:S(2)}) collective-permute-start(bf16[256,8,256]{0,2,1:T(8,128)(2,1)} %pad_maximum_fusion.2), channel_id=1, source_target_pairs={{2,0},{3,1},{4,2},{5,3},{6,4},{7,5},{8,6},{9,7},{10,8},{11,9},{12,... | collective-permute-start | bytes 3145736 | tf_op jit(solution)/shard_map/ppermute | solution.py:24
  208.6 102.4 %collective-permute-start.4 = (bf16[256,8,256]{0,2,1:T(8,128)(2,1)}, bf16[256,8,256]{0,2,1:T(8,128)(2,1)S(1)}, u32[]{:S(2)}, u32[]{:S(2)}) collective-permute-start(bf16[256,8,256]{0,2,1:T(8,128)(2,1)} %pad_maximum_fusion.1), channel_id=1, source_target_pairs={{1,0},{2,1},{3,2},{4,3},{5,4},{6,5},{7,6},{8,7},{9,8},{10,9},{11,1... | collective-permute-start | bytes 3145736 | tf_op jit(solution)/shard_map/ppermute | solution.py:24
Sparse Core Ops, SparseCore 0:
  28.6 50.1 reduce-scatter.3
  193.9 41.0 all-gather.2

commit v2 on v1

--- a/solution.py
+++ b/solution.py
@@ -58,60 +58,78 @@
     return (normed.astype(jnp.bfloat16), score_grad)
 
 
+def chunk_mask(query_start, key_start, tokens):
+    query_pos = query_start + lax.iota(jnp.int32, tokens)
+    key_pos = key_start + lax.iota(jnp.int32, tokens)
+    distance = query_pos[:, None] - key_pos[None, :]
+    return (key_pos[None, :] >= 0) & (distance >= 0) & (distance < WINDOW)
+
+
 def on_device(
     query_rows, key_rows, value_rows, out_grad, gate_grads, first_moment, second_moment, master_rows
 ):
     tokens = query_rows.shape[1]
     group_size = HEADS // KV_HEADS
-    ctx_count = lax.axis_size("ctx")
     ctx_index = lax.axis_index("ctx")
     reach = (WINDOW - 1) // tokens + 1
-    seq_len = tokens * ctx_count
     query_heads = query_rows[0].reshape(tokens, KV_HEADS, group_size, HEAD_DIM)
     grad_heads = out_grad[0].reshape(tokens, KV_HEADS, group_size, HEAD_DIM)
     key_heads = key_rows[0].reshape(tokens, KV_HEADS, HEAD_DIM)
     value_heads = value_rows[0].reshape(tokens, KV_HEADS, HEAD_DIM)
     packed = jnp.concatenate([key_heads, value_heads], axis=2)
-    key_list = []
-    value_list = []
-    for offset in range(reach, 0, -1):
+    chunk_keys = {0: key_heads}
+    chunk_values = {0: value_heads}
+    for offset in range(1, reach + 1):
         shifted = passed_along(packed, "ctx", offset)
-        key_list.append(shifted[:, :, :HEAD_DIM])
-        value_list.append(shifted[:, :, HEAD_DIM:])
-    key_all = jnp.concatenate(key_list + [key_heads], axis=0)
-    value_all = jnp.concatenate(value_list + [value_heads], axis=0)
-    visible, query_live = window_mask(
-        ctx_index * tokens, (ctx_index - reach) * tokens, tokens, (reach + 1) * tokens, seq_len
-    )
-    capped, weights = capped_weights(query_heads, key_all, visible)
-    totals = jnp.sum(weights.astype(jnp.float32), axis=3)
-    weighted = jnp.einsum("grab,bgd->agrd", weights, value_all, preferred_element_type=jnp.float32)
+        chunk_keys[offset] = shifted[:, :, :HEAD_DIM]
+        chunk_values[offset] = shifted[:, :, HEAD_DIM:]
+    query_start = ctx_index * tokens
+    capped = {}
+    weights = {}
+    totals = None
+    weighted = None
+    for c in range(reach + 1):
+        visible = chunk_mask(query_start, (ctx_index - c) * tokens, tokens)
+        capped[c], weights[c] = capped_weights(query_heads, chunk_keys[c], visible)
+        part_total = jnp.sum(weights[c].astype(jnp.float32), axis=3)
+        part_weighted = jnp.einsum(
+            "grab,bgd->agrd", weights[c], chunk_values[c], preferred_element_type=jnp.float32
+        )
+        totals = part_total if totals is None else totals + part_total
+        weighted = part_weighted if weighted is None else weighted + part_weighted
     attended = (weighted / jnp.transpose(totals, (2, 0, 1))[..., None]).astype(jnp.bfloat16)
     deltas = jnp.transpose(
         jnp.sum(grad_heads.astype(jnp.float32) * attended.astype(jnp.float32), axis=3), (1, 2, 0)
     )
-    rounded, score_grad = score_terms(grad_heads, value_all, capped, weights, totals, deltas)
-    query_grad = (
-        jnp.einsum("grab,bgd->agrd", score_grad, key_all, preferred_element_type=jnp.float32)
-        * SCORE_SCALE
-    ).astype(jnp.bfloat16)
-    key_part = jnp.einsum(
-        "grab,agrd->bgd", score_grad, query_heads, preferred_element_type=jnp.float32
-    )
-    value_part = jnp.einsum(
-        "grab,agrd->bgd", rounded, grad_heads, preferred_element_type=jnp.float32
-    )
-    key_acc = key_part[reach * tokens :]
-    value_acc = value_part[reach * tokens :]
-    for offset in range(1, reach + 1):
-        first_row = (reach - offset) * tokens
-        outgoing = jnp.concatenate(
-            [key_part[first_row : first_row + tokens], value_part[first_row : first_row + tokens]],
-            axis=2,
-        ).astype(jnp.bfloat16)
-        returned = passed_along(outgoing, "ctx", -offset).astype(jnp.float32)
-        key_acc = key_acc + returned[:, :, :HEAD_DIM]
-        value_acc = value_acc + returned[:, :, HEAD_DIM:]
+    query_acc = None
+    key_acc = None
+    value_acc = None
+    for c in range(reach, -1, -1):
+        rounded, score_grad = score_terms(
+            grad_heads, chunk_values[c], capped[c], weights[c], totals, deltas
+        )
+        part_query = jnp.einsum(
+            "grab,bgd->agrd", score_grad, chunk_keys[c], preferred_element_type=jnp.float32
+        )
+        query_acc = part_query if query_acc is None else query_acc + part_query
+        key_part = jnp.einsum(
+            "grab,agrd->bgd", score_grad, query_heads, preferred_element_type=jnp.float32
+        )
+        value_part = jnp.einsum(
+            "grab,agrd->bgd", rounded, grad_heads, preferred_element_type=jnp.float32
+        )
+        if c == 0:
+            own_key, own_value = key_part, value_part
+            continue
+        outgoing = jnp.concatenate([key_part, value_part], axis=2).astype(jnp.bfloat16)
+        returned = passed_along(outgoing, "ctx", -c).astype(jnp.float32)
+        key_acc = returned[:, :, :HEAD_DIM] if key_acc is None else key_acc + returned[:, :, :HEAD_DIM]
+        value_acc = (
+            returned[:, :, HEAD_DIM:] if value_acc is None else value_acc + returned[:, :, HEAD_DIM:]
+        )
+    key_acc = own_key + key_acc
+    value_acc = own_value + value_acc
+    query_grad = (query_acc * SCORE_SCALE).astype(jnp.bfloat16)
     query_out = query_grad.reshape(1, tokens, HEADS * HEAD_DIM)
     key_out = (key_acc * SCORE_SCALE).astype(jnp.bfloat16).reshape(1, tokens, KV_HEADS * HEAD_DIM)
     value_out = value_acc.astype(jnp.bfloat16).reshape(1, tokens, KV_HEADS * HEAD_DIM)

time: 328 us -> 292 us (0.89)
  waiting for transfers between devices: 178 us -> 146 us
  local copies, waits for them, and re-layouts: 24.6 us -> 19.3 us
    ppermute x8, waiting for transfers between devices: 178 us -> 146 us  [passed_along(): return lax.ppermute(block, axis, route)]
    dot_general x2 -> x10, matrix products: 16.3 us -> 24.1 us  [the longest x5 12.6 us: on_device(): jnp.einsum('grab,bgd->agrd', score_grad, chunk_keys[c], preferred_element...]
    dot_general x1 -> x5, matrix products: 12.3 us -> 8.34 us  [on_device(): jnp.einsum('grab,agrd->bgd', rounded, grad_heads, preferred_element_type=...]
    dot_general x1 -> x5, matrix products: 9.83 us -> 7.05 us  [on_device(): jnp.einsum('grab,agrd->bgd', score_grad, query_heads, preferred_element_t...]
    unnamed x27 -> x51, local copies, waits for them, and re-layouts: 17.8 us -> 15.1 us
    dot_general x1 -> x5, matrix products: 10.2 us -> 11.1 us  [capped_weights(): jnp.einsum('agrd,bgd->grab', query_heads, key_heads, preferred_element_ty...]
    convert_element_type x5 -> x4, other arithmetic: 6.99 us -> 6.4 us  [on_device(): returned = passed_along(outgoing, 'ctx', -c).astype(jnp.float32)]
    dot_general x1 -> x5, matrix products: 15.6 us -> 15.5 us  [score_terms(): jnp.einsum('agrd,bgd->grab', grad_heads, value_heads, preferred_element_t...]
  transfers between devices with their start and end apart: 10 -> 10, of which waited for: 8 -> 6; matrix products, arithmetic and copies ran while one was open for 29% -> 32% of each run, Pallas kernels for 0% -> 0%
where the time goes in v2:
time: 292 us; the launch traced here: 289 us
  waiting for transfers between devices  146 us (50%)
  matrix products  66.1 us (23%)
  starting transfers between devices  26.1 us (9%)
  local copies, waits for them, and re-layouts  19.3 us (7%)
  other arithmetic  16 us (5%)
  between operations  15.1 us (5%)
    ppermute x8, waiting for transfers between devices, passed_along(): return lax.ppermute(block, axis, route)  146 us
    ppermute x8, starting transfers between devices, passed_along(): return lax.ppermute(block, axis, route)  26 us
    dot_general x5, matrix products, score_terms(): jnp.einsum('agrd,bgd->grab', grad_heads, value_heads, preferred_element_t...  15.5 us
    unnamed x51, local copies, waits for them, and re-layouts  15.1 us
    dot_general x5, matrix products, on_device(): jnp.einsum('grab,bgd->agrd', score_grad, chunk_keys[c], preferred_element...  12.6 us
    dot_general x5, matrix products, on_device(): jnp.einsum('grab,bgd->agrd', weights[c], chunk_values[c], preferred_eleme...  11.4 us
    dot_general x5, matrix products, capped_weights(): jnp.einsum('agrd,bgd->grab', query_heads, key_heads, preferred_element_ty...  11.1 us
    dot_general x5, matrix products, on_device(): jnp.einsum('grab,agrd->bgd', rounded, grad_heads, preferred_element_type=...  8.34 us
  transfers between devices with their start and end apart: 10, of which 6 were waited for; matrix products, arithmetic and copies ran while one was open for 32% of the time, Pallas kernels for 0%

profile of v2, /device:TPU:248, one launch (start us, length us, event | category | flops | bytes accessed | tf_op | source)
XLA Modules:
  0.0 288.5 jit_solution(11082954117798961970)
XLA Ops:
  7.2 1.3 copy.118
  8.9 1.2 copy.119
  10.4 1.1 pad_maximum_fusion
  11.5 4.7 %collective-permute-start = (bf16[256,8,256]{2,0,1:T(8,128)(2,1)}, bf16[256,8,256]{2,0,1:T(8,128)(2,1)}, u32[]{:S(2)}, u32[]{:S(2)}) collective-permute-start(bf16[256,8,256]{2,0,1:T(8,128)(2,1)} %pad_maximum_fusion), channel_id=1, source_target_pairs={{0,4},{1,5},{2,6},{3,7},{4,8},{5,9},{6,10},{7,11},{8,12},{9,13},{1... | collective-permute-start | bytes 3145736 | tf_op jit(solution)/shard_map/ppermute | solution.py:24
  16.2 3.1 %collective-permute-start.3 = (bf16[256,8,256]{2,0,1:T(8,128)(2,1)}, bf16[256,8,256]{2,0,1:T(8,128)(2,1)}, u32[]{:S(2)}, u32[]{:S(2)}) collective-permute-start(bf16[256,8,256]{2,0,1:T(8,128)(2,1)} %pad_maximum_fusion), channel_id=1, source_target_pairs={{0,3},{1,4},{2,5},{3,6},{4,7},{5,8},{6,9},{7,10},{8,11},{9,12},{10... | collective-permute-start | bytes 3145736 | tf_op jit(solution)/shard_map/ppermute | solution.py:24
  19.3 3.3 %collective-permute-start.2 = (bf16[256,8,256]{2,0,1:T(8,128)(2,1)}, bf16[256,8,256]{2,0,1:T(8,128)(2,1)}, u32[]{:S(2)}, u32[]{:S(2)}) collective-permute-start(bf16[256,8,256]{2,0,1:T(8,128)(2,1)} %pad_maximum_fusion), channel_id=1, source_target_pairs={{0,2},{1,3},{2,4},{3,5},{4,6},{5,7},{6,8},{7,9},{8,10},{9,11},{10,... | collective-permute-start | bytes 3145736 | tf_op jit(solution)/shard_map/ppermute | solution.py:24
  22.7 4.1 %collective-permute-start.1 = (bf16[256,8,256]{2,0,1:T(8,128)(2,1)}, bf16[256,8,256]{2,0,1:T(8,128)(2,1)}, u32[]{:S(2)}, u32[]{:S(2)}) collective-permute-start(bf16[256,8,256]{2,0,1:T(8,128)(2,1)} %pad_maximum_fusion), channel_id=1, source_target_pairs={{0,1},{1,2},{2,3},{3,4},{4,5},{5,6},{6,7},{7,8},{8,9},{9,10},{10,1... | collective-permute-start | bytes 3145736 | tf_op jit(solution)/shard_map/ppermute | solution.py:24
  26.8 1.7 copy.247
  28.6 1.6 copy.249
  30.2 1.3 copy.128
  32.3 1.4 convert_reduce_fusion.3
  33.8 1.4 fusion.112
  35.2 4.9 %collective-permute-done = bf16[256,8,256]{2,0,1:T(8,128)(2,1)} collective-permute-done((bf16[256,8,256]{2,0,1:T(8,128)(2,1)}, bf16[256,8,256]{2,0,1:T(8,128)(2,1)}, u32[]{:S(2)}, u32[]{:S(2)}) %collective-permute-start) | collective-permute-done | bytes 1048608 | tf_op jit(solution)/shard_map/ppermute | solution.py:24
  40.1 2.5 convert_reduce_fusion.4
  42.5 27.7 %collective-permute-done.3 = bf16[256,8,256]{2,0,1:T(8,128)(2,1)} collective-permute-done((bf16[256,8,256]{2,0,1:T(8,128)(2,1)}, bf16[256,8,256]{2,0,1:T(8,128)(2,1)}, u32[]{:S(2)}, u32[]{:S(2)}) %collective-permute-start.3) | collective-permute-done | bytes 1048608 | tf_op jit(solution)/shard_map/ppermute | solution.py:24
  70.3 2.4 convert_reduce_fusion
  72.7 22.1 %collective-permute-done.2 = bf16[256,8,256]{2,0,1:T(8,128)(2,1)} collective-permute-done((bf16[256,8,256]{2,0,1:T(8,128)(2,1)}, bf16[256,8,256]{2,0,1:T(8,128)(2,1)}, u32[]{:S(2)}, u32[]{:S(2)}) %collective-permute-start.2) | collective-permute-done | bytes 1048608 | tf_op jit(solution)/shard_map/ppermute | solution.py:24
  94.8 2.4 convert_reduce_fusion.1
  97.2 29.4 %collective-permute-done.1 = bf16[256,8,256]{2,0,1:T(8,128)(2,1)} collective-permute-done((bf16[256,8,256]{2,0,1:T(8,128)(2,1)}, bf16[256,8,256]{2,0,1:T(8,128)(2,1)}, u32[]{:S(2)}, u32[]{:S(2)}) %collective-permute-start.1) | collective-permute-done | bytes 1048608 | tf_op jit(solution)/shard_map/ppermute | solution.py:24
  126.6 2.5 convert_reduce_fusion.2
  129.1 1.4 fusion.69
  130.6 1.4 fusion.78
  132.0 1.4 fusion.75
  133.4 1.6 fusion.72
  135.1 2.4 fusion.96
  137.5 2.4 fusion.97
  139.9 2.4 fusion.98
  142.3 2.9 multiply_reduce_fusion
  145.2 3.2 %fusion.8 = bf16[8,2,256,256]{2,3,1,0:T(8,128)(2,1)S(1)} fusion(f32[8,256,256,2]{2,1,3,0:T(8,128)S(1)} %get-tuple-element.38, bf16[256,8,2,128]{0,3,2,1:T(8,128)(2,1)S(1)} %bitcast.415, f32[8,2,256]{2,1,0:T(2,128)S(1)} %bitcast.439, f32[8,2,256]{2,1,0:T(2,128)S(1)} %bitcast.428, bf16[256,8,256]{2,0,1:T(8,128)(2,1)} %collective-permute-done, ...), kind=kOutput, calls=%fused_computation.27 | convolution fusion | flops 281018368 | bytes 7962624 | tf_op jit(solution)/shard_map/agrd,bgd->grab/dot_general | solution.py:52
  148.4 0.8 fusion.68
  149.3 1.1 pad_maximum_fusion.1
  150.4 1.9 collective-permute-start.4
  152.3 3.2 %fusion.6 = bf16[8,2,256,256]{2,3,1,0:T(8,128)(2,1)S(1)} fusion(f32[8,256,256,2]{2,1,3,0:T(8,128)S(1)} %get-tuple-element.40, bf16[256,8,2,128]{0,3,2,1:T(8,128)(2,1)S(1)} %bitcast.416, f32[8,2,256]{2,1,0:T(2,128)S(1)} %bitcast.440, f32[8,2,256]{2,1,0:T(2,128)S(1)} %bitcast.429, bf16[256,8,256]{2,0,1:T(8,128)(2,1)} %collective-permute-done.3, ...), kind=kOutput, calls=%fused_computation.23 | convolution fusion | flops 281018368 | bytes 7962624 | tf_op jit(solution)/shard_map/agrd,bgd->grab/dot_general | solution.py:52
  155.5 0.8 fusion.67
  156.4 1.1 pad_maximum_fusion.2
  157.4 4.1 %collective-permute-start.5 = (bf16[256,8,256]{0,2,1:T(8,128)(2,1)}, bf16[256,8,256]{0,2,1:T(8,128)(2,1)}, u32[]{:S(2)}, u32[]{:S(2)}) collective-permute-start(bf16[256,8,256]{0,2,1:T(8,128)(2,1)} %pad_maximum_fusion.2), channel_id=1, source_target_pairs={{3,0},{4,1},{5,2},{6,3},{7,4},{8,5},{9,6},{10,7},{11,8},{12,9},{13... | collective-permute-start | bytes 3145736 | tf_op jit(solution)/shard_map/ppermute | solution.py:24
  161.6 3.2 %fusion.4 = bf16[8,2,256,256]{2,3,1,0:T(8,128)(2,1)S(1)} fusion(f32[8,256,256,2]{2,1,3,0:T(8,128)S(1)} %get-tuple-element.42, bf16[256,8,2,128]{0,3,2,1:T(8,128)(2,1)S(1)} %bitcast.417, f32[8,2,256]{2,1,0:T(2,128)S(1)} %bitcast.441, f32[8,2,256]{2,1,0:T(2,128)S(1)} %bitcast.430, bf16[256,8,256]{2,0,1:T(8,128)(2,1)} %collective-permute-done.2, ...), kind=kOutput, calls=%fused_computation.19 | convolution fusion | flops 281018368 | bytes 7962624 | tf_op jit(solution)/shard_map/agrd,bgd->grab/dot_general | solution.py:52
  165.6 1.0 pad_maximum_fusion.3
  166.7 1.9 collective-permute-start.6
  168.6 3.5 %fusion.2 = bf16[8,2,256,256]{2,3,1,0:T(8,128)(2,1)S(1)} fusion(f32[8,256,256,2]{2,1,3,0:T(8,128)S(1)} %get-tuple-element.46, bf16[256,8,2,128]{0,3,2,1:T(8,128)(2,1)S(1)} %bitcast.418, f32[8,2,256]{2,1,0:T(2,128)S(1)} %bitcast.442, f32[8,2,256]{2,1,0:T(2,128)S(1)} %bitcast.431, bf16[256,8,256]{2,0,1:T(8,128)(2,1)} %collective-permute-done.1, ...), kind=kOutput, calls=%fused_computation.15 | convolution fusion | flops 281018368 | bytes 7962624 | tf_op jit(solution)/shard_map/agrd,bgd->grab/dot_general | solution.py:52
  172.1 0.8 fusion.65
  172.9 1.1 pad_maximum_fusion.4
  174.0 2.9 collective-permute-start.7
  176.9 2.3 fusion
  179.3 2.0 fusion.124
  181.3 3.0 %fusion.94 = f32[8,128,2,256]{3,1,2,0:T(8,128)} fusion(bf16[8,2,256,256]{2,3,1,0:T(8,128)(2,1)S(1)} %fusion.6, bf16[256,8,256]{2,0,1:T(8,128)(2,1)} %collective-permute-done.3), kind=kOutput, calls=%fused_computation.126 | convolution fusion | flops 268435456 | bytes 4718592 | tf_op jit(solution)/shard_map/grab,bgd->agrd/dot_general | solution.py:111
  184.2 2.9 fusion.89
  187.1 1.2 copy.248
  188.3 3.3 %convert_bitcast_fusion = (bf16[1,576,288]{1,2,0:T(8,128)(2,1)}, f32[288,576]{1,0:T(8,128)}, f32[288,576]{1,0:T(8,128)}, f32[288,576]{1,0:T(8,128)}) fusion(f32[288,576]{1,0:T(8,128)} %param.15, bf16[288,576]{1,0:T(8,128)(2,1)S(1)} %copy.248, f32[288,576]{1,0:T(8,128)} %param.13, f32[288,576]{1,0:T(8,128)} %param.14), kind=kLoop, calls=%fused_computation.141 | loop fusion | flops 2322432 | bytes 4644864
  191.7 1.7 fusion.92
  194.1 3.2 %fusion.21 = bf16[256,8,2,128]{0,3,2,1:T(8,128)(2,1)S(1)} fusion(f32[8,2,256,128]{2,3,1,0:T(8,128)S(1)} %copy-done.4, f32[8,128,2,256]{3,1,2,0:T(8,128)S(1)} %fusion.92, f32[8,128,2,256]{3,1,2,0:T(8,128)} %fusion.89, f32[8,128,2,256]{3,1,2,0:T(8,128)} %fusion.94, bf16[8,2,256,256]{2,3,1,0:T(8,128)(2,1)S(1)} %copy-done.1, ...), kind=kOutput, calls=%fused_computation.52 | convolution fusion | flops 271581184 | bytes 12058624 | tf_op jit(solution)/shard_map/grab,bgd->agrd/dot_general | solution.py:111
  197.2 1.4 copy.169
  198.7 1.4 convert_element_type.127
  200.1 2.2 convert_element_type.129
  202.3 2.7 collective-permute-done.6
  205.1 1.4 convert_element_type.131
  206.5 58.9 %collective-permute-done.7 = bf16[256,8,256]{0,2,1:T(8,128)(2,1)} collective-permute-done((bf16[256,8,256]{0,2,1:T(8,128)(2,1)}, bf16[256,8,256]{0,2,1:T(8,128)(2,1)}, u32[]{:S(2)}, u32[]{:S(2)}) %collective-permute-start.7) | collective-permute-done | bytes 1048608 | tf_op jit(solution)/shard_map/ppermute | solution.py:24
  265.4 1.4 convert_element_type.133
  266.9 2.4 fusion.82
  269.2 2.0 copy.171
  271.3 3.8 %fusion.85 = bf16[256,8,128]{0,2,1:T(8,128)(2,1)} fusion(f32[256,8,256]{0,2,1:T(8,128)} %copy-done.8, f32[256,8,256]{0,2,1:T(8,128)} %copy-done.7, f32[256,8,256]{0,2,1:T(8,128)} %copy-done.6, f32[256,8,256]{0,2,1:T(8,128)} %copy-done.5, bf16[8,2,256,256]{2,3,1,0:T(8,128)(2,1)S(1)} %copy-done.3, bf16[256,8,2,128]{0,3,2,1:T(8,128)(2,1)S(1)} %bitcast.398), kind=kOutput, calls=%fused_computation.100 | convolution fusion | flops 270008320 | bytes 7864320 | tf_op jit(solution)/shard_map/grab,agrd->bgd/dot_general | solution.py:115
  275.1 2.0 copy.170
  277.1 2.1 copy.168
  279.2 2.0 reshape.312
  (61 shorter events, 3.0 us)
Async XLA Ops:
  7.2 19.6 %copy-start.13 = (bf16[1,288,2304]{2,1,0:T(8,128)(2,1)S(1)}, bf16[1,288,2304]{2,1,0:T(8,128)(2,1)}, u32[]{:S(2)}) copy-start(bf16[1,288,2304]{2,1,0:T(8,128)(2,1)} %param.12) | copy-start | bytes 3981316
  7.2 179.9 %reduce-scatter.4.cloned.1.call-start = ((), (), s32[]{:S(2)}) async-start(), calls=%async_computation.2 | async-start | bytes 2211840
  8.6 23.7 %copy-start.9 = (bf16[1,256,1024]{1,2,0:T(8,128)(2,1)}, bf16[1,256,1024]{1,2,0:T(8,128)(2,1)S(1)}, u32[]{:S(2)}) copy-start(bf16[1,256,1024]{1,2,0:T(8,128)(2,1)S(1)} %copy.118) | copy-start | bytes 1572868
  10.1 23.7 %copy-start.11 = (bf16[1,256,1024]{1,2,0:T(8,128)(2,1)}, bf16[1,256,1024]{1,2,0:T(8,128)(2,1)S(1)}, u32[]{:S(2)}) copy-start(bf16[1,256,1024]{1,2,0:T(8,128)(2,1)S(1)} %copy.119) | copy-start | bytes 1572868
  11.5 28.6 %collective-permute-start = (bf16[256,8,256]{2,0,1:T(8,128)(2,1)}, bf16[256,8,256]{2,0,1:T(8,128)(2,1)}, u32[]{:S(2)}, u32[]{:S(2)}) collective-permute-start(bf16[256,8,256]{2,0,1:T(8,128)(2,1)} %pad_maximum_fusion), channel_id=1, source_target_pairs={{0,4},{1,5},{2,6},{3,7},{4,8},{5,9},{6,10},{7,11},{8,12},{9,13},{1... | collective-permute-start | bytes 3145736 | tf_op jit(solution)/shard_map/ppermute | solution.py:24
  16.2 54.1 %collective-permute-start.3 = (bf16[256,8,256]{2,0,1:T(8,128)(2,1)}, bf16[256,8,256]{2,0,1:T(8,128)(2,1)}, u32[]{:S(2)}, u32[]{:S(2)}) collective-permute-start(bf16[256,8,256]{2,0,1:T(8,128)(2,1)} %pad_maximum_fusion), channel_id=1, source_target_pairs={{0,3},{1,4},{2,5},{3,6},{4,7},{5,8},{6,9},{7,10},{8,11},{9,12},{10... | collective-permute-start | bytes 3145736 | tf_op jit(solution)/shard_map/ppermute | solution.py:24
  19.3 75.4 %collective-permute-start.2 = (bf16[256,8,256]{2,0,1:T(8,128)(2,1)}, bf16[256,8,256]{2,0,1:T(8,128)(2,1)}, u32[]{:S(2)}, u32[]{:S(2)}) collective-permute-start(bf16[256,8,256]{2,0,1:T(8,128)(2,1)} %pad_maximum_fusion), channel_id=1, source_target_pairs={{0,2},{1,3},{2,4},{3,5},{4,6},{5,7},{6,8},{7,9},{8,10},{9,11},{10,... | collective-permute-start | bytes 3145736 | tf_op jit(solution)/shard_map/ppermute | solution.py:24
  22.7 103.9 %collective-permute-start.1 = (bf16[256,8,256]{2,0,1:T(8,128)(2,1)}, bf16[256,8,256]{2,0,1:T(8,128)(2,1)}, u32[]{:S(2)}, u32[]{:S(2)}) collective-permute-start(bf16[256,8,256]{2,0,1:T(8,128)(2,1)} %pad_maximum_fusion), channel_id=1, source_target_pairs={{0,1},{1,2},{2,3},{3,4},{4,5},{5,6},{6,7},{7,8},{8,9},{9,10},{10,1... | collective-permute-start | bytes 3145736 | tf_op jit(solution)/shard_map/ppermute | solution.py:24
  28.4 1.8 copy-start.14
  28.5 248.6 %all-gather.3.cloned.1.call-start = ((), (), s32[]{:S(2)}) async-start(), calls=%async_computation.1 | async-start | bytes 1843200 | tf_op jit(solution)/shard_map/all_gather | solution.py:147
  32.3 144.6 %copy-start.17 = (pred[256,256]{0,1:T(8,128)(4,1)}, pred[256,256]{0,1:T(8,128)(4,1)S(1)}, u32[]{:S(2)}) copy-start(pred[256,256]{0,1:T(8,128)(4,1)S(1)} %get-tuple-element.35) | copy-start | bytes 196612
  33.8 143.2 %copy-start.19 = (f32[8,256,256,2]{2,1,3,0:T(8,128)}, f32[8,256,256,2]{2,1,3,0:T(8,128)S(1)}, u32[]{:S(2)}) copy-start(f32[8,256,256,2]{2,1,3,0:T(8,128)S(1)} %get-tuple-element.44) | copy-start | bytes 12582916
  126.6 2.5 copy-start.15
  150.4 48.3 %collective-permute-start.4 = (bf16[256,8,256]{0,2,1:T(8,128)(2,1)}, bf16[256,8,256]{0,2,1:T(8,128)(2,1)}, u32[]{:S(2)}, u32[]{:S(2)}) collective-permute-start(bf16[256,8,256]{0,2,1:T(8,128)(2,1)} %pad_maximum_fusion.1), channel_id=1, source_target_pairs={{4,0},{5,1},{6,2},{7,3},{8,4},{9,5},{10,6},{11,7},{12,8},{13,9},{1... | collective-permute-start | bytes 3145736 | tf_op jit(solution)/shard_map/ppermute | solution.py:24
  157.4 42.7 %collective-permute-start.5 = (bf16[256,8,256]{0,2,1:T(8,128)(2,1)}, bf16[256,8,256]{0,2,1:T(8,128)(2,1)}, u32[]{:S(2)}, u32[]{:S(2)}) collective-permute-start(bf16[256,8,256]{0,2,1:T(8,128)(2,1)} %pad_maximum_fusion.2), channel_id=1, source_target_pairs={{3,0},{4,1},{5,2},{6,3},{7,4},{8,5},{9,6},{10,7},{11,8},{12,9},{13... | collective-permute-start | bytes 3145736 | tf_op jit(solution)/shard_map/ppermute | solution.py:24
  166.7 38.4 %collective-permute-start.6 = (bf16[256,8,256]{0,2,1:T(8,128)(2,1)}, bf16[256,8,256]{0,2,1:T(8,128)(2,1)}, u32[]{:S(2)}, u32[]{:S(2)}) collective-permute-start(bf16[256,8,256]{0,2,1:T(8,128)(2,1)} %pad_maximum_fusion.3), channel_id=1, source_target_pairs={{2,0},{3,1},{4,2},{5,3},{6,4},{7,5},{8,6},{9,7},{10,8},{11,9},{12,... | collective-permute-start | bytes 3145736 | tf_op jit(solution)/shard_map/ppermute | solution.py:24
  172.1 7.2 %copy-start = (bf16[8,2,256,256]{2,3,1,0:T(8,128)(2,1)}, bf16[8,2,256,256]{2,3,1,0:T(8,128)(2,1)S(1)}, u32[]{:S(2)}) copy-start(bf16[8,2,256,256]{2,3,1,0:T(8,128)(2,1)S(1)} %fusion.2) | copy-start | bytes 6291460
  172.1 4.8 %copy-start.12 = (bf16[1,256,1024]{1,2,0:T(8,128)(2,1)S(1)}, bf16[1,256,1024]{1,2,0:T(8,128)(2,1)}, u32[]{:S(2)}) copy-start(bf16[1,256,1024]{1,2,0:T(8,128)(2,1)} %copy-done.11) | copy-start | bytes 1572868
  174.0 5.2 %copy-start.10 = (bf16[1,256,1024]{1,2,0:T(8,128)(2,1)S(1)}, bf16[1,256,1024]{1,2,0:T(8,128)(2,1)}, u32[]{:S(2)}) copy-start(bf16[1,256,1024]{1,2,0:T(8,128)(2,1)} %copy-done.9) | copy-start | bytes 1572868
  174.0 91.3 %collective-permute-start.7 = (bf16[256,8,256]{0,2,1:T(8,128)(2,1)}, bf16[256,8,256]{0,2,1:T(8,128)(2,1)}, u32[]{:S(2)}, u32[]{:S(2)}) collective-permute-start(bf16[256,8,256]{0,2,1:T(8,128)(2,1)} %pad_maximum_fusion.4), channel_id=1, source_target_pairs={{1,0},{2,1},{3,2},{4,3},{5,4},{6,5},{7,6},{8,7},{9,8},{10,9},{11,1... | collective-permute-start | bytes 3145736 | tf_op jit(solution)/shard_map/ppermute | solution.py:24
  179.3 4.9 %copy-start.2 = (bf16[8,2,256,256]{2,3,1,0:T(8,128)(2,1)}, bf16[8,2,256,256]{2,3,1,0:T(8,128)(2,1)S(1)}, u32[]{:S(2)}) copy-start(bf16[8,2,256,256]{2,3,1,0:T(8,128)(2,1)S(1)} %fusion) | copy-start | bytes 6291460
  191.7 1.7 copy-start.1
  191.7 2.4 copy-start.4
  200.1 66.7 %copy-start.5 = (f32[256,8,256]{0,2,1:T(8,128)}, f32[256,8,256]{0,2,1:T(8,128)S(1)}, u32[]{:S(2)}) copy-start(f32[256,8,256]{0,2,1:T(8,128)S(1)} %convert_element_type.127) | copy-start | bytes 6291460
  200.1 66.7 %copy-start.16 = (bf16[1,256,2048]{1,2,0:T(8,128)(2,1)S(1)}, bf16[1,256,2048]{1,2,0:T(8,128)(2,1)}, u32[]{:S(2)}) copy-start(bf16[1,256,2048]{1,2,0:T(8,128)(2,1)} %copy.128) | copy-start | bytes 3145732
  200.1 66.7 %copy-start.18 = (pred[256,256]{0,1:T(8,128)(4,1)S(1)}, pred[256,256]{0,1:T(8,128)(4,1)}, u32[]{:S(2)}) copy-start(pred[256,256]{0,1:T(8,128)(4,1)} %copy-done.17) | copy-start | bytes 196612
  200.1 66.7 %copy-start.20 = (f32[8,256,256,2]{2,1,3,0:T(8,128)S(1)}, f32[8,256,256,2]{2,1,3,0:T(8,128)}, u32[]{:S(2)}) copy-start(f32[8,256,256,2]{2,1,3,0:T(8,128)} %copy-done.19) | copy-start | bytes 12582916
  202.3 66.9 %copy-start.6 = (f32[256,8,256]{0,2,1:T(8,128)}, f32[256,8,256]{0,2,1:T(8,128)S(1)}, u32[]{:S(2)}) copy-start(f32[256,8,256]{0,2,1:T(8,128)S(1)} %convert_element_type.129) | copy-start | bytes 6291460
  206.5 62.7 %copy-start.7 = (f32[256,8,256]{0,2,1:T(8,128)}, f32[256,8,256]{0,2,1:T(8,128)S(1)}, u32[]{:S(2)}) copy-start(f32[256,8,256]{0,2,1:T(8,128)S(1)} %convert_element_type.131) | copy-start | bytes 6291460
  266.8 2.4 copy-start.8
  266.8 4.4 %copy-start.3 = (bf16[8,2,256,256]{2,3,1,0:T(8,128)(2,1)S(1)}, bf16[8,2,256,256]{2,3,1,0:T(8,128)(2,1)}, u32[]{:S(2)}) copy-start(bf16[8,2,256,256]{2,3,1,0:T(8,128)(2,1)} %copy-done.2) | copy-start | bytes 6291460
Sparse Core Ops, SparseCore 0:
  28.6 50.1 reduce-scatter.3
  191.8 35.8 all-gather.2
